TPU v7x, 256 devices: a whole 4x4x8 slice. The times are simulated.
256 devices in a mesh: slab: 32 (over z, x), coil: 8 (over y, core).
Axes of the slice: x: 4, y: 4, z: 8, core: 2. Of those that a mesh axis runs over, the one named last changes fastest.
Arguments:
- noisy: float32 [2, 64, 256, 128], P(None, 'slab', 'coil'), may hold values from -6 to 6
- step_index: int32 [], replicated, may hold values from 200 to 599
- w_in: bfloat16 [3, 3, 3, 32, 2], replicated, may hold values from -0.875 to 0.875
- w_mid: bfloat16 [3, 3, 3, 32, 32], replicated, may hold values from -0.21875 to 0.21875
- w_out: bfloat16 [3, 3, 3, 2, 32], replicated, may hold values from -0.21875 to 0.21875
- time_weight: float32 [32, 32], replicated, may hold values from -1 to 1
- sens: float32 [16, 2, 64, 256, 128], P('coil', None, 'slab')
- kdata: float32 [16, 2, 64, 256, 128], P('coil', None, None, 'slab'), may hold values from -4 to 4
- mask: int32 [64, 256], P(None, 'slab'), may hold values from 0 to 1, as said below
Outputs:
- recon: float32 [2, 64, 256, 128], P(None, 'slab', 'coil')
- next_sample: float32 [2, 64, 256, 128], P(None, 'slab', 'coil')
Inputs may be any that keep to these rules, and one draw needn't show every extreme that they name: mask[kz, ky] is 1 wherever min(kz, 64 - kz) < max(1, 4) and min(ky, 256 - ky) < max(1, 8); every other entry is 1 with chance one in three.
All inputs are finite; a program needn't handle non-finite values.
Results may differ from a plain program's by a relative error of at most 0.0023.
Values may be sent and summed in bfloat16 or wider, within the bound.
No kernel may reach another device: no remote copies, remote signals or barrier semaphores. Data moves between devices by JAX's collectives and lax.ppermute only.
A program may use at most 64 MiB of HBM per device.

v0:
```python
import math
import jax
import jax.numpy as jnp
from jax import lax
from jax.sharding import PartitionSpec as P

ITERS = 2
STEPS = 1000
STRIDE = 20
REG_WEIGHT = 0.5
HIGHEST_PRECISION = lax.Precision.HIGHEST


def extended(cells, sides, width):
    for axis, dim in sides:
        count = lax.axis_size(axis)
        ends = count - 1
        head = lax.slice_in_dim(cells, 0, width, axis=dim)
        tail = lax.slice_in_dim(cells, cells.shape[dim] - width, cells.shape[dim], axis=dim)
        cells = jnp.concatenate(
            [
                lax.ppermute(tail, axis, [(i, (i + 1) % count) for i in range(ends)]),
                cells,
                lax.ppermute(head, axis, [((i + 1) % count, i) for i in range(ends)]),
            ],
            axis=dim,
        )
    return cells


def plan_level(step_value):
    angle = (step_value / STEPS + 0.008) / 1.008 * (math.pi / 2)
    return jnp.cos(angle) ** 2


def time_bias(step_value, time_weight):
    half = time_weight.shape[0] // 2
    freqs = jnp.exp(-math.log(10000.0) * jnp.arange(half, dtype=jnp.float32) / half)
    phase = step_value * freqs
    embed = jnp.concatenate([jnp.sin(phase), jnp.cos(phase)])
    return jnp.dot(embed, time_weight, precision=HIGHEST_PRECISION)


def conv_layer(inputs, weights):
    padded = extended(inputs, (("slab", 1), ("coil", 2)), 1)
    kernel = jnp.transpose(weights, (3, 4, 0, 1, 2))
    result = lax.conv_general_dilated(
        padded[None],
        kernel,
        (1, 1, 1),
        ((0, 0), (0, 0), (1, 1)),
        dimension_numbers=("NCDHW", "OIDHW", "NCDHW"),
        preferred_element_type=jnp.float32,
    )
    return result[0]


def dft_blocks(length, inverse):
    index = jnp.arange(length, dtype=jnp.int32)
    product = index[:, None] * index[None, :] % length
    theta = product.astype(jnp.float32) * (2.0 * math.pi / length)
    cosine = jnp.cos(theta) / math.sqrt(length)
    sine = jnp.sin(theta) / math.sqrt(length)
    if inverse:
        sine = -sine
    upper = jnp.stack([cosine, sine], axis=1)
    lower = jnp.stack([-sine, cosine], axis=1)
    return jnp.stack([upper, lower], axis=0)


def along_last(data, blocks):
    return jnp.einsum("pkqn,cqzyn->cpzyk", blocks, data, precision=HIGHEST_PRECISION)


def along_rows(data, blocks):
    return jnp.einsum("pkqn,cqzny->cpzky", blocks, data, precision=HIGHEST_PRECISION)


def along_depth(data, blocks):
    return jnp.einsum("pkqn,cqnyx->cpkyx", blocks, data, precision=HIGHEST_PRECISION)


def times_sens(sens, image):
    real_part = sens[:, 0] * image[0] - sens[:, 1] * image[1]
    imag_part = sens[:, 0] * image[1] + sens[:, 1] * image[0]
    return jnp.stack([real_part, imag_part], axis=1)


def times_conj(sens, images):
    real_part = jnp.sum(sens[:, 0] * images[:, 0] + sens[:, 1] * images[:, 1], axis=0)
    imag_part = jnp.sum(sens[:, 0] * images[:, 1] - sens[:, 1] * images[:, 0], axis=0)
    return jnp.stack([real_part, imag_part])


def coil_term(image_full, sens, kdata_x, weight, blocks, with_data):
    forward_y, forward_z, inverse_y, inverse_z = blocks
    coil_images = times_sens(sens, image_full)
    spectrum = along_rows(coil_images, forward_y)
    pencils = lax.all_to_all(
        spectrum.astype(jnp.bfloat16), "slab", split_axis=3, concat_axis=2, tiled=True
    ).astype(jnp.float32)
    kspace = along_depth(pencils, forward_z)
    if with_data:
        kspace = weight * (kdata_x - kspace)
    else:
        kspace = weight * kspace
    back = along_depth(kspace, inverse_z)
    slabs = lax.all_to_all(
        back.astype(jnp.bfloat16), "slab", split_axis=2, concat_axis=3, tiled=True
    ).astype(jnp.float32)
    images = along_rows(slabs, inverse_y)
    return times_conj(sens, images)


def combine_coils(partial_value):
    count = lax.axis_size("coil")
    pieces = lax.all_to_all(partial_value, "coil", split_axis=2, concat_axis=0, tiled=True)
    pieces = pieces.reshape((count, partial_value.shape[0]) + pieces.shape[1:])
    return jnp.sum(pieces, axis=0)


def gather_rows(value):
    return lax.all_gather(value, "coil", axis=2, tiled=True)


def global_sums(values):
    axes = ("slab", "coil")
    count = lax.axis_size("slab") * lax.axis_size("coil")
    spread = jnp.broadcast_to(values[None], (count,) + values.shape)
    return jnp.sum(lax.all_to_all(spread, axes, split_axis=0, concat_axis=0, tiled=True), axis=0)


def body(noisy, step_index, w_in, w_mid, w_out, time_weight, sens, kdata, mask):
    step_value = step_index.astype(jnp.float32)
    signal_level = plan_level(step_value)
    prior_level = plan_level(step_value - STRIDE)
    bias = time_bias(step_value, time_weight)
    hidden = jax.nn.silu(
        conv_layer(noisy.astype(jnp.bfloat16), w_in) + bias[:, None, None, None]
    ).astype(jnp.bfloat16)
    mixed = (hidden.astype(jnp.float32) + jax.nn.silu(conv_layer(hidden, w_mid))).astype(
        jnp.bfloat16
    )
    noise_pred = conv_layer(mixed, w_out)
    estimate = (noisy - jnp.sqrt(1.0 - signal_level) * noise_pred) / jnp.sqrt(signal_level)
    depth_full = kdata.shape[2]
    rows_full = sens.shape[3]
    width = sens.shape[4]
    blocks = (
        dft_blocks(rows_full, False),
        dft_blocks(depth_full, False),
        dft_blocks(rows_full, True),
        dft_blocks(depth_full, True),
    )
    kdata_x = along_last(kdata, dft_blocks(width, True))
    weight = mask.astype(jnp.float32)[None, None, :, :, None]

    def operator(image, with_data):
        return combine_coils(
            coil_term(gather_rows(image), sens, kdata_x, weight, blocks, with_data)
        )

    solution = estimate
    residual = operator(estimate, True)
    direction = residual
    norm_now = None
    for iteration in range(ITERS):
        final_turn = iteration + 1 == ITERS
        image = operator(direction, False) + REG_WEIGHT * direction
        if norm_now is None:
            sums = global_sums(
                jnp.stack([jnp.sum(residual * residual), jnp.sum(direction * image)])
            )
            norm_now, curvature = (sums[0], sums[1])
        else:
            curvature = global_sums(jnp.stack([jnp.sum(direction * image)]))[0]
        step_size = norm_now / curvature
        solution = solution + step_size * direction
        if not final_turn:
            residual = residual - step_size * image
            norm_next = global_sums(jnp.stack([jnp.sum(residual * residual)]))[0]
            direction = residual + norm_next / norm_now * direction
            norm_now = norm_next
    recon = solution
    next_sample = jnp.sqrt(prior_level) * recon + jnp.sqrt(1.0 - prior_level) * noise_pred
    return (recon, next_sample)


def solution(mesh):
    return jax.shard_map(
        body,
        mesh=mesh,
        in_specs=(
            P(None, "slab", "coil", None),
            P(),
            P(),
            P(),
            P(),
            P(),
            P("coil", None, "slab", None, None),
            P("coil", None, None, "slab", None),
            P(None, "slab"),
        ),
        out_specs=(P(None, "slab", "coil", None), P(None, "slab", "coil", None)),
        check_vma=False,
    )
```

profile of v0, /device:TPU:1, one launch (start us, length us, event | category | flops | bytes accessed | tf_op | source)
XLA Modules:
  0.0 684.9 jit_solution(6342718819612224770)
XLA Ops:
  22.7 7.8 %broadcast_select_fusion.1 = f32[2,32,8,17,32]{4,2,3,1,0:T(8,128)S(1)} fusion(pred[8,17]{0,1:T(8,128)(4,1)} %constant.113, bf16[3,3,3,32,2]{3,4,2,1,0:T(2,128)(2,1)} %param.11, bf16[2,4,34,1,7,2]{4,0,5,2,1,3:T(2,128)(2,1)S(1)} %slice.155, bf16[2,4,34,1,8,17]{4,0,5,2,1,3:T(2,128)(2,1)S(1)} %copy.378), kind=kOutput, calls=%fused_computation.23 | convolution fusion | flops 30607616 | bytes 1199304 | tf_op jit(solution)/shard_map/conv_general_dilated | solution.py:47
  75.3 8.1 %copy.497 = bf16[32,4,34,1,128]{2,0,4,1,3:T(8,128)(2,1)} copy(bf16[32,4,34,1,128]{0,2,4,1,3:T(8,128)(2,1)} %maximum_bitcast_fusion) | data formatting | bytes 2228224
  88.5 8.7 %copy.386 = bf16[32,4,34,1,8,17]{0,4,5,2,1,3:T(8,128)(2,1)} copy(bf16[32,4,34,1,8,17]{2,0,5,4,1,3:T(8,128)(2,1)} %bitcast.328) | data formatting | bytes 2367488 | tf_op jit(solution)/shard_map/conv_general_dilated | solution.py:47
  98.5 8.6 %broadcast_select_fusion = f32[2,32,8,17,32]{4,2,3,1,0:T(8,128)S(1)} fusion(pred[8,17]{0,1:T(8,128)(4,1)S(1)} %copy-done.25, bf16[3,3,3,32,32]{4,3,2,1,0:T(8,128)(2,1)S(1)} %copy-done.26, bf16[32,4,34,1,7,2]{0,4,5,2,1,3:T(8,128)(2,1)S(1)} %slice.159, bf16[32,4,34,1,8,17]{0,4,5,2,1,3:T(8,128)(2,1)} %copy.386), kind=kOutput, calls=%fused_computation.22 | convolution fusion | flops 485543936 | bytes 2475144 | tf_op jit(solution)/shard_map/conv_general_dilated | solution.py:47
  156.4 8.1 %copy.498 = bf16[32,4,34,1,128]{2,0,4,1,3:T(8,128)(2,1)} copy(bf16[32,4,34,1,128]{0,2,4,1,3:T(8,128)(2,1)} %maximum_bitcast_fusion.1) | data formatting | bytes 2228224
  169.6 8.7 %copy.394 = bf16[32,4,34,1,8,17]{0,4,5,2,1,3:T(8,128)(2,1)} copy(bf16[32,4,34,1,8,17]{2,0,5,4,1,3:T(8,128)(2,1)} %bitcast.327) | data formatting | bytes 2367488 | tf_op jit(solution)/shard_map/conv_general_dilated | solution.py:47
  179.5 139.8 %fusion.11 = f32[2,32,8,17,2]{2,4,3,1,0:T(2,128)} fusion(bf16[3,3,3,2,32]{4,3,2,1,0:T(2,128)(2,1)S(1)} %copy-done.27, bf16[32,4,34,1,7,2]{0,4,5,2,1,3:T(8,128)(2,1)S(1)} %slice.163, bf16[32,4,34,1,8,17]{0,4,5,2,1,3:T(8,128)(2,1)} %copy.394), kind=kOutput, calls=%fused_computation.11 | convolution fusion | flops 34050048 | bytes 1378688 | tf_op jit(solution)/shard_map/conv_general_dilated | solution.py:47
  325.5 14.1 %all_gather.9 = f32[2,2,256,128]{3,1,0,2:T(2,128)S(1)} all-gather(f32[2,2,32,128]{3,1,0,2:T(2,128)S(1)} %fusion.74), channel_id=1, replica_groups=mesh['slab'=32,'coil'=8] {'coil'}, dimensions={2}, use_global_device_ids=true | all-gather | bytes 589824 | tf_op jit(solution)/shard_map/all_gather | solution.py:123
  350.0 14.7 %all-to-all-start = ((bf16[2,2,2,256,128]{4,1,2,0,3:T(2,128)(2,1)}), bf16[2,2,2,256,128]{4,1,2,0,3:T(2,128)(2,1)S(1)}, u32[]{:S(2)}, u32[]{:S(2)}) async-start(bf16[2,2,2,256,128]{4,1,2,0,3:T(2,128)(2,1)} %copy.404), calls=%async_computation | async-start | bytes 1048576 | tf_op jit(solution)/shard_map/all_to_all | solution.py:99
  369.0 12.5 %all-to-all-done = bf16[2,2,2,256,128]{4,1,2,0,3:T(2,128)(2,1)S(1)} async-done(((bf16[2,2,2,256,128]{4,1,2,0,3:T(2,128)(2,1)}), bf16[2,2,2,256,128]{4,1,2,0,3:T(2,128)(2,1)S(1)}, u32[]{:S(2)}, u32[]{:S(2)}) %all-to-all-start) | async-done | bytes 524320 | tf_op jit(solution)/shard_map/all_to_all | solution.py:99
  385.3 20.3 %all_to_all.162 = bf16[2,2,64,8,128]{4,1,3,0,2:T(2,128)(2,1)S(1)} all-to-all(bf16[2,2,64,8,128]{4,1,3,0,2:T(2,128)(2,1)S(1)} %copy.408), channel_id=1, replica_groups=mesh['slab'=32,'coil'=8] {'slab'}, dimensions={2} | all-to-all | bytes 1048576 | tf_op jit(solution)/shard_map/all_to_all | solution.py:108
  410.0 16.8 %all_to_all.163 = f32[2,2,256,128]{3,1,0,2:T(2,128)} all-to-all(f32[2,2,256,128]{3,1,0,2:T(2,128)} %copy.412), channel_id=1, replica_groups=mesh['slab'=32,'coil'=8] {'coil'}, dimensions={2} | all-to-all | bytes 1048576 | tf_op jit(solution)/shard_map/all_to_all | solution.py:117
  428.1 14.2 %all_gather.10 = f32[2,2,256,128]{3,1,0,2:T(2,128)S(1)} all-gather(f32[2,2,32,128]{3,1,0,2:T(2,128)S(1)} %reduce_sum.146), channel_id=1, replica_groups=mesh['slab'=32,'coil'=8] {'coil'}, dimensions={2}, use_global_device_ids=true | all-gather | bytes 589824 | tf_op jit(solution)/shard_map/all_gather | solution.py:123
  453.8 21.1 %all_to_all.164 = bf16[2,2,2,256,128]{4,1,2,0,3:T(2,128)(2,1)S(1)} all-to-all(bf16[2,2,2,256,128]{4,1,2,0,3:T(2,128)(2,1)} %copy.415), channel_id=1, replica_groups=mesh['slab'=32,'coil'=8] {'slab'}, dimensions={3} | all-to-all | bytes 1048576 | tf_op jit(solution)/shard_map/all_to_all | solution.py:99
  478.3 20.3 %all_to_all.165 = bf16[2,2,64,8,128]{4,1,3,0,2:T(2,128)(2,1)S(1)} all-to-all(bf16[2,2,64,8,128]{4,1,3,0,2:T(2,128)(2,1)S(1)} %copy.419), channel_id=1, replica_groups=mesh['slab'=32,'coil'=8] {'slab'}, dimensions={2} | all-to-all | bytes 1048576 | tf_op jit(solution)/shard_map/all_to_all | solution.py:108
  503.0 16.8 %all_to_all.166 = f32[2,2,256,128]{3,1,0,2:T(2,128)} all-to-all(f32[2,2,256,128]{3,1,0,2:T(2,128)} %copy.423), channel_id=1, replica_groups=mesh['slab'=32,'coil'=8] {'coil'}, dimensions={2} | all-to-all | bytes 1048576 | tf_op jit(solution)/shard_map/all_to_all | solution.py:117
  523.3 19.5 %all_to_all.167 = f32[256,1,2]{2,1,0:T(1,128)} all-to-all(f32[256,1,2]{2,1,0:T(1,128)S(1)} %broadcast_in_dim.15), channel_id=1, replica_groups=mesh['slab'=32,'coil'=8] {'slab','coil'}, dimensions={0} | all-to-all | bytes 4096 | tf_op jit(solution)/shard_map/all_to_all | solution.py:130
  548.7 19.5 %all_to_all.168 = f32[256,1,1]{2,1,0:T(1,128)} all-to-all(f32[256,1,1]{2,1,0:T(1,128)S(1)} %broadcast_in_dim.16), channel_id=1, replica_groups=mesh['slab'=32,'coil'=8] {'slab','coil'}, dimensions={0} | all-to-all | bytes 2048 | tf_op jit(solution)/shard_map/all_to_all | solution.py:130
  572.2 13.6 %all_gather.11 = f32[2,2,256,128]{3,1,0,2:T(2,128)S(1)} all-gather(f32[2,2,32,128]{3,1,0,2:T(2,128)S(1)} %multiply_add_fusion.4), channel_id=1, replica_groups=mesh['slab'=32,'coil'=8] {'coil'}, dimensions={2}, use_global_device_ids=true | all-gather | bytes 589824 | tf_op jit(solution)/shard_map/all_gather | solution.py:123
  597.4 21.0 %all_to_all.169 = bf16[2,2,2,256,128]{4,1,2,0,3:T(2,128)(2,1)S(1)} all-to-all(bf16[2,2,2,256,128]{4,1,2,0,3:T(2,128)(2,1)} %copy.428), channel_id=1, replica_groups=mesh['slab'=32,'coil'=8] {'slab'}, dimensions={3} | all-to-all | bytes 1048576 | tf_op jit(solution)/shard_map/all_to_all | solution.py:99
  621.8 20.3 %all_to_all.170 = bf16[2,2,64,8,128]{4,1,3,0,2:T(2,128)(2,1)S(1)} all-to-all(bf16[2,2,64,8,128]{4,1,3,0,2:T(2,128)(2,1)S(1)} %copy.432), channel_id=1, replica_groups=mesh['slab'=32,'coil'=8] {'slab'}, dimensions={2} | all-to-all | bytes 1048576 | tf_op jit(solution)/shard_map/all_to_all | solution.py:108
  644.0 15.2 %all_to_all.171 = f32[2,2,256,128]{3,1,0,2:T(2,128)S(1)} all-to-all(f32[2,2,256,128]{3,1,0,2:T(2,128)S(1)} %copy.436), channel_id=1, replica_groups=mesh['slab'=32,'coil'=8] {'coil'}, dimensions={2} | all-to-all | bytes 1048576 | tf_op jit(solution)/shard_map/all_to_all | solution.py:117
  661.4 6.5 all-to-all-start.11
  668.3 12.6 %all-to-all-done.11 = f32[256,1,1]{2,1,0:T(1,128)S(1)} async-done(((f32[256,1,1]{2,1,0:T(1,128)}), f32[256,1,1]{2,1,0:T(1,128)S(1)}, u32[]{:S(2)}, u32[]{:S(2)}) %all-to-all-start.11) | async-done | bytes 1056 | tf_op jit(solution)/shard_map/all_to_all | solution.py:130
  (206 shorter events, 209.2 us)
Async XLA Ops:
  0.6 366.3 %copy-start = (f32[2,2,64,8,128]{4,3,2,1,0:T(8,128)S(1)}, f32[2,2,64,8,128]{4,3,2,1,0:T(8,128)}, u32[]{:S(2)}) copy-start(f32[2,2,64,8,128]{4,3,2,1,0:T(8,128)} %param.16) | copy-start | bytes 3145732
  1.6 5.9 collective-permute-start
  5.5 4.5 collective-permute-start.1
  10.0 8.1 %collective-permute-start.2 = (bf16[2,4,1,128]{3,2,1,0:T(2,128)(2,1)S(1)}, bf16[2,4,1,128]{3,2,1,0:T(2,128)(2,1)S(1)}, u32[]{:S(2)}, u32[]{:S(2)}) collective-permute-start(bf16[2,4,1,128]{3,2,1,0:T(2,128)(2,1)S(1)} %get-tuple-element.62), channel_id=1, source_target_pairs={{0,1},{1,2},{2,3},{3,4},{4,5},{5,6},{6,7},{8,9},{9,10},{10,11},{11... | collective-permute-start | bytes 6152 | tf_op jit(solution)/shard_map/ppermute | solution.py:22
  15.2 4.9 collective-permute-start.3
  36.8 10.5 %collective-permute-start.4 = (bf16[32,1,32,128]{3,2,1,0:T(8,128)(2,1)S(1)}, bf16[32,1,32,128]{3,2,1,0:T(8,128)(2,1)}, u32[]{:S(2)}, u32[]{:S(2)}) collective-permute-start(bf16[32,1,32,128]{3,2,1,0:T(8,128)(2,1)S(1)} %copy.380), channel_id=1, source_target_pairs={{0,8},{8,16},{16,24},{24,32},{32,40},{40,48},{48,56},{56,64},{64,7... | collective-permute-start | bytes 786440 | tf_op jit(solution)/shard_map/ppermute | solution.py:22
  44.2 9.1 %collective-permute-start.5 = (bf16[32,1,32,128]{3,2,1,0:T(8,128)(2,1)}, bf16[32,1,32,128]{3,2,1,0:T(8,128)(2,1)}, u32[]{:S(2)}, u32[]{:S(2)}) collective-permute-start(bf16[32,1,32,128]{3,2,1,0:T(8,128)(2,1)} %copy.381), channel_id=1, source_target_pairs={{8,0},{16,8},{24,16},{32,24},{40,32},{48,40},{56,48},{64,56},{72,6... | collective-permute-start | bytes 786440 | tf_op jit(solution)/shard_map/ppermute | solution.py:24
  58.9 7.7 %collective-permute-start.6 = (bf16[32,4,1,128]{0,2,3,1:T(2,128)(2,1)S(1)}, bf16[32,4,1,128]{0,2,3,1:T(2,128)(2,1)S(1)}, u32[]{:S(2)}, u32[]{:S(2)}) collective-permute-start(bf16[32,4,1,128]{0,2,3,1:T(2,128)(2,1)S(1)} %get-tuple-element.28), channel_id=1, source_target_pairs={{0,1},{1,2},{2,3},{3,4},{4,5},{5,6},{6,7},{8,9},{9,10},{10,11},{11... | collective-permute-start | bytes 98312 | tf_op jit(solution)/shard_map/ppermute | solution.py:22
  63.0 7.7 %collective-permute-start.7 = (bf16[32,4,1,128]{0,2,3,1:T(2,128)(2,1)S(1)}, bf16[32,4,1,128]{0,2,3,1:T(2,128)(2,1)S(1)}, u32[]{:S(2)}, u32[]{:S(2)}) collective-permute-start(bf16[32,4,1,128]{0,2,3,1:T(2,128)(2,1)S(1)} %get-tuple-element.29), channel_id=1, source_target_pairs={{1,0},{2,1},{3,2},{4,3},{5,4},{6,5},{7,6},{9,8},{10,9},{11,10},{12... | collective-permute-start | bytes 98312 | tf_op jit(solution)/shard_map/ppermute | solution.py:24
  115.4 11.5 %collective-permute-start.8 = (bf16[32,1,32,128]{3,2,1,0:T(8,128)(2,1)}, bf16[32,1,32,128]{3,2,1,0:T(8,128)(2,1)}, u32[]{:S(2)}, u32[]{:S(2)}) collective-permute-start(bf16[32,1,32,128]{3,2,1,0:T(8,128)(2,1)} %copy.388), channel_id=1, source_target_pairs={{0,8},{8,16},{16,24},{24,32},{32,40},{40,48},{48,56},{56,64},{64,7... | collective-permute-start | bytes 786440 | tf_op jit(solution)/shard_map/ppermute | solution.py:22
  123.2 7.6 %collective-permute-start.9 = (bf16[32,1,32,128]{3,2,1,0:T(8,128)(2,1)}, bf16[32,1,32,128]{3,2,1,0:T(8,128)(2,1)}, u32[]{:S(2)}, u32[]{:S(2)}) collective-permute-start(bf16[32,1,32,128]{3,2,1,0:T(8,128)(2,1)} %copy.389), channel_id=1, source_target_pairs={{8,0},{16,8},{24,16},{32,24},{40,32},{48,40},{56,48},{64,56},{72,6... | collective-permute-start | bytes 786440 | tf_op jit(solution)/shard_map/ppermute | solution.py:24
  137.0 12.9 %collective-permute-start.10 = (bf16[32,4,1,128]{0,2,3,1:T(2,128)(2,1)}, bf16[32,4,1,128]{0,2,3,1:T(2,128)(2,1)}, u32[]{:S(2)}, u32[]{:S(2)}) collective-permute-start(bf16[32,4,1,128]{0,2,3,1:T(2,128)(2,1)} %get-tuple-element.26), channel_id=1, source_target_pairs={{0,1},{1,2},{2,3},{3,4},{4,5},{5,6},{6,7},{8,9},{9,10},{10,11},{11... | collective-permute-start | bytes 98312 | tf_op jit(solution)/shard_map/ppermute | solution.py:22
  142.1 8.0 %collective-permute-start.11 = (bf16[32,4,1,128]{0,2,3,1:T(2,128)(2,1)}, bf16[32,4,1,128]{0,2,3,1:T(2,128)(2,1)}, u32[]{:S(2)}, u32[]{:S(2)}) collective-permute-start(bf16[32,4,1,128]{0,2,3,1:T(2,128)(2,1)} %get-tuple-element.27), channel_id=1, source_target_pairs={{1,0},{2,1},{3,2},{4,3},{5,4},{6,5},{7,6},{9,8},{10,9},{11,10},{12... | collective-permute-start | bytes 98312 | tf_op jit(solution)/shard_map/ppermute | solution.py:24
  319.3 24.9 %copy-start.2 = (f32[2,1,2,256,128]{3,4,1,2,0:T(8,128)S(1)}, f32[2,1,2,256,128]{3,4,1,2,0:T(8,128)}, u32[]{:S(2)}) copy-start(f32[2,1,2,256,128]{3,4,1,2,0:T(8,128)} %copy.490) | copy-start | bytes 1572868
  319.3 24.9 %copy-start.3 = (f32[2,1,2,256,128]{3,4,1,2,0:T(8,128)S(1)}, f32[2,1,2,256,128]{3,4,1,2,0:T(8,128)}, u32[]{:S(2)}) copy-start(f32[2,1,2,256,128]{3,4,1,2,0:T(8,128)} %copy.492) | copy-start | bytes 1572868
  319.3 26.1 %copy-start.8 = (f32[1,256,2,256]{3,1,2,0:T(8,128)S(1)}, f32[1,256,2,256]{3,1,2,0:T(8,128)}, u32[]{:S(2)}) copy-start(f32[1,256,2,256]{3,1,2,0:T(8,128)} %get-tuple-element.46) | copy-start | bytes 1572868
  319.3 26.1 %copy-start.9 = (f32[1,256,2,256]{3,1,2,0:T(8,128)S(1)}, f32[1,256,2,256]{3,1,2,0:T(8,128)}, u32[]{:S(2)}) copy-start(f32[1,256,2,256]{3,1,2,0:T(8,128)} %get-tuple-element.55) | copy-start | bytes 1572868
  325.5 24.5 %copy-start.22 = (f32[2,2,32,128]{3,1,0,2:T(2,128)}, f32[2,2,32,128]{3,1,0,2:T(2,128)S(1)}, u32[]{:S(2)}) copy-start(f32[2,2,32,128]{3,1,0,2:T(2,128)S(1)} %fusion.74) | copy-start | bytes 196612
  340.6 24.1 %copy-start.24 = (s32[64,8]{0,1:T(8,128)S(1)}, s32[64,8]{0,1:T(8,128)}, u32[]{:S(2)}) copy-start(s32[64,8]{0,1:T(8,128)} %param.17) | copy-start | bytes 6148
  350.0 31.4 %all-to-all-start = ((bf16[2,2,2,256,128]{4,1,2,0,3:T(2,128)(2,1)}), bf16[2,2,2,256,128]{4,1,2,0,3:T(2,128)(2,1)S(1)}, u32[]{:S(2)}, u32[]{:S(2)}) async-start(bf16[2,2,2,256,128]{4,1,2,0,3:T(2,128)(2,1)} %copy.404), calls=%async_computation | async-start | bytes 1048576 | tf_op jit(solution)/shard_map/all_to_all | solution.py:99
  366.9 108.2 %copy-start.14 = (f32[1,64,2,64]{3,1,2,0:T(8,128)}, f32[1,64,2,64]{3,1,2,0:T(8,128)S(1)}, u32[]{:S(2)}) copy-start(f32[1,64,2,64]{3,1,2,0:T(8,128)S(1)} %get-tuple-element.57) | copy-start | bytes 98308
  521.0 49.0 %copy-start.10 = (f32[2,2,32,128]{3,1,0,2:T(2,128)}, f32[2,2,32,128]{3,1,0,2:T(2,128)S(1)}, u32[]{:S(2)}) copy-start(f32[2,2,32,128]{3,1,0,2:T(2,128)S(1)} %reduce_sum.150) | copy-start | bytes 196612
  643.4 39.7 %copy-start.23 = (f32[2,2,32,128]{3,1,0,2:T(2,128)S(1)}, f32[2,2,32,128]{3,1,0,2:T(2,128)}, u32[]{:S(2)}) copy-start(f32[2,2,32,128]{3,1,0,2:T(2,128)} %copy-done.22) | copy-start | bytes 196612
  661.4 19.5 %all-to-all-start.11 = ((f32[256,1,1]{2,1,0:T(1,128)}), f32[256,1,1]{2,1,0:T(1,128)S(1)}, u32[]{:S(2)}, u32[]{:S(2)}) async-start(f32[256,1,1]{2,1,0:T(1,128)} %broadcast_in_dim.17), calls=%async_computation.11 | async-start | bytes 262144 | tf_op jit(solution)/shard_map/all_to_all | solution.py:130
  (20 other events, 290.6 us)
where the time goes:
time: 697 us; the launch traced here: 685 us
  blocking collectives  233 us (33%)
  matrix products  181 us (26%)
  local copies, waits for them, and re-layouts  123 us (18%)
  starting transfers between devices  57.9 us (8%)
  other arithmetic  46.4 us (7%)
  waiting for transfers between devices  36.7 us (5%)
    conv_general_dilated x3, matrix products, conv_layer(): lax.conv_general_dilated(padded[None], kernel, (1, 1, 1), ((0, 0), (0, 0)...  156 us
    all_to_all x3, blocking collectives, coil_term(): lax.all_to_all(back.astype(jnp.bfloat16), 'slab', split_axis=2, concat_ax...  60.9 us
    all_to_all x3, blocking collectives, combine_coils(): lax.all_to_all(partial_value, 'coil', split_axis=2, concat_axis=0, tiled=...  48.8 us
    all_to_all x2, blocking collectives, coil_term(): lax.all_to_all(spectrum.astype(jnp.bfloat16), 'slab', split_axis=3, conca...  42.1 us
    all_gather x3, blocking collectives, gather_rows(): return lax.all_gather(value, 'coil', axis=2, tiled=True)  42 us
    all_to_all x2, blocking collectives, global_sums(): lax.all_to_all(spread, axes, split_axis=0, concat_axis=0, tiled=True)  39 us
    ppermute x6, starting transfers between devices, extended(): lax.ppermute(tail, axis, [(i, (i + 1) % count) for i in range(ends)])  27 us
    conv_general_dilated x9, local copies, waits for them, and re-layouts, conv_layer(): lax.conv_general_dilated(padded[None], kernel, (1, 1, 1), ((0, 0), (0, 0)...  26 us
  transfers between devices with their start and end apart: 14, of which 8 were waited for; matrix products, arithmetic and copies ran while one was open for 4% of the time, Pallas kernels for 0%

commit v1 on v0

--- a/solution.py
+++ b/solution.py
@@ -9,6 +9,10 @@
 STRIDE = 20
 REG_WEIGHT = 0.5
 HIGHEST_PRECISION = lax.Precision.HIGHEST
+balance_face = lambda field, dim_i: jnp.concatenate(
+    lax.all_to_all(jnp.stack([field for _ in range(lax.axis_size("coil"))], axis=0), "coil", 0, 0),
+    axis=dim_i,
+)
 
 
 def extended(cells, sides, width):
@@ -120,7 +124,7 @@
 
 
 def gather_rows(value):
-    return lax.all_gather(value, "coil", axis=2, tiled=True)
+    return balance_face(value, dim_i=2)
 
 
 def global_sums(values):

time: 697 us -> 689 us (0.989)
  blocking collectives: 233 us -> 217 us
  waiting for transfers between devices: 36.7 us -> 50.6 us
    all_gather x3 -> x0, blocking collectives: 42 us -> none  [gather_rows(): return lax.all_gather(value, 'coil', axis=2, tiled=True)]
    all_to_all x0 -> x2, blocking collectives: none -> 25.6 us  [lax.all_to_all(jnp.stack([field for _ in range(lax.axis_size('coil'))], a...]
    ppermute x6, waiting for transfers between devices: 11.5 us -> 20.1 us  [extended(): lax.ppermute(head, axis, [((i + 1) % count, i) for i in range(ends)])]
    unnamed x69 -> x53, local copies, waits for them, and re-layouts: 23.1 us -> 19 us
  transfers between devices with their start and end apart: 14 -> 15, of which waited for: 8 -> 11; matrix products, arithmetic and copies ran while one was open for 4% -> 4% of each run, Pallas kernels for 0% -> 0%
where the time goes in v1:
time: 689 us; the launch traced here: 678 us
  blocking collectives  217 us (31%)
  matrix products  182 us (26%)
  local copies, waits for them, and re-layouts  117 us (17%)
  starting transfers between devices  61.9 us (9%)
  waiting for transfers between devices  50.6 us (7%)
  other arithmetic  42.6 us (6%)
    conv_general_dilated x3, matrix products, conv_layer(): lax.conv_general_dilated(padded[None], kernel, (1, 1, 1), ((0, 0), (0, 0)...  155 us
    all_to_all x3, blocking collectives, coil_term(): lax.all_to_all(back.astype(jnp.bfloat16), 'slab', split_axis=2, concat_ax...  63.5 us
    all_to_all x3, blocking collectives, combine_coils(): lax.all_to_all(partial_value, 'coil', split_axis=2, concat_axis=0, tiled=...  49.4 us
    all_to_all x2, blocking collectives, coil_term(): lax.all_to_all(spectrum.astype(jnp.bfloat16), 'slab', split_axis=3, conca...  39.3 us
    all_to_all x2, blocking collectives, global_sums(): lax.all_to_all(spread, axes, split_axis=0, concat_axis=0, tiled=True)  39.1 us
    ppermute x6, starting transfers between devices, extended(): lax.ppermute(tail, axis, [(i, (i + 1) % count) for i in range(ends)])  27 us
    all_to_all x2, blocking collectives, lax.all_to_all(jnp.stack([field for _ in range(lax.axis_size('coil'))], a...  25.6 us
    conv_general_dilated x9, local copies, waits for them, and re-layouts, conv_layer(): lax.conv_general_dilated(padded[None], kernel, (1, 1, 1), ((0, 0), (0, 0)...  24.2 us
  transfers between devices with their start and end apart: 15, of which 11 were waited for; matrix products, arithmetic and copies ran while one was open for 4% of the time, Pallas kernels for 0%

profile of v1, /device:TPU:1, one launch (start us, length us, event | category | flops | bytes accessed | tf_op | source)
XLA Modules:
  0.0 677.8 jit_solution(5427869748281032894)
XLA Ops:
  22.7 7.8 %broadcast_select_fusion.1 = f32[2,32,8,17,32]{4,2,3,1,0:T(8,128)S(1)} fusion(pred[8,17]{0,1:T(8,128)(4,1)} %constant.113, bf16[3,3,3,32,2]{3,4,2,1,0:T(2,128)(2,1)} %param.11, bf16[2,4,34,1,7,2]{4,0,5,2,1,3:T(2,128)(2,1)S(1)} %slice.161, bf16[2,4,34,1,8,17]{4,0,5,2,1,3:T(2,128)(2,1)S(1)} %copy.408), kind=kOutput, calls=%fused_computation.23 | convolution fusion | flops 30607616 | bytes 1199304 | tf_op jit(solution)/shard_map/conv_general_dilated | solution.py:51
  75.3 8.1 %copy.533 = bf16[32,4,34,1,128]{2,0,4,1,3:T(8,128)(2,1)} copy(bf16[32,4,34,1,128]{0,2,4,1,3:T(8,128)(2,1)} %maximum_bitcast_fusion) | data formatting | bytes 2228224
  88.6 8.7 %copy.416 = bf16[32,4,34,1,8,17]{0,4,5,2,1,3:T(8,128)(2,1)} copy(bf16[32,4,34,1,8,17]{2,0,5,4,1,3:T(8,128)(2,1)} %bitcast.331) | data formatting | bytes 2367488 | tf_op jit(solution)/shard_map/conv_general_dilated | solution.py:51
  98.6 8.6 %broadcast_select_fusion = f32[2,32,8,17,32]{4,2,3,1,0:T(8,128)S(1)} fusion(pred[8,17]{0,1:T(8,128)(4,1)S(1)} %copy-done.17, bf16[3,3,3,32,32]{4,3,2,1,0:T(8,128)(2,1)S(1)} %copy-done.18, bf16[32,4,34,1,7,2]{0,4,5,2,1,3:T(8,128)(2,1)S(1)} %slice.165, bf16[32,4,34,1,8,17]{0,4,5,2,1,3:T(8,128)(2,1)} %copy.416), kind=kOutput, calls=%fused_computation.22 | convolution fusion | flops 485543936 | bytes 2475144 | tf_op jit(solution)/shard_map/conv_general_dilated | solution.py:51
  149.3 6.3 maximum_bitcast_fusion.1
  155.6 8.1 %copy.534 = bf16[32,4,34,1,128]{2,0,4,1,3:T(8,128)(2,1)} copy(bf16[32,4,34,1,128]{0,2,4,1,3:T(8,128)(2,1)} %maximum_bitcast_fusion.1) | data formatting | bytes 2228224
  168.8 8.7 %copy.424 = bf16[32,4,34,1,8,17]{0,4,5,2,1,3:T(8,128)(2,1)} copy(bf16[32,4,34,1,8,17]{2,0,5,4,1,3:T(8,128)(2,1)} %bitcast.330) | data formatting | bytes 2367488 | tf_op jit(solution)/shard_map/conv_general_dilated | solution.py:51
  178.7 138.9 %fusion.11 = f32[2,32,8,17,2]{2,4,3,1,0:T(2,128)S(1)} fusion(bf16[3,3,3,2,32]{4,3,2,1,0:T(2,128)(2,1)S(1)} %copy-done.19, bf16[32,4,34,1,7,2]{0,4,5,2,1,3:T(8,128)(2,1)S(1)} %slice.169, bf16[32,4,34,1,8,17]{0,4,5,2,1,3:T(8,128)(2,1)} %copy.424), kind=kOutput, calls=%fused_computation.11 | convolution fusion | flops 34050048 | bytes 1378688 | tf_op jit(solution)/shard_map/conv_general_dilated | solution.py:51
  345.5 14.8 %all-to-all-start.1 = ((bf16[2,2,2,256,128]{4,1,2,0,3:T(2,128)(2,1)}), bf16[2,2,2,256,128]{4,1,2,0,3:T(2,128)(2,1)}, u32[]{:S(2)}, u32[]{:S(2)}) async-start(bf16[2,2,2,256,128]{4,1,2,0,3:T(2,128)(2,1)} %copy.436), calls=%async_computation.1 | async-start | bytes 1048576 | tf_op jit(solution)/shard_map/all_to_all | solution.py:103
  364.6 11.2 %all-to-all-done.1 = bf16[2,2,2,256,128]{4,1,2,0,3:T(2,128)(2,1)} async-done(((bf16[2,2,2,256,128]{4,1,2,0,3:T(2,128)(2,1)}), bf16[2,2,2,256,128]{4,1,2,0,3:T(2,128)(2,1)}, u32[]{:S(2)}, u32[]{:S(2)}) %all-to-all-start.1) | async-done | bytes 524320 | tf_op jit(solution)/shard_map/all_to_all | solution.py:103
  380.6 21.4 %all_to_all.177 = bf16[2,2,64,8,128]{4,1,3,0,2:T(2,128)(2,1)S(1)} all-to-all(bf16[2,2,64,8,128]{4,1,3,0,2:T(2,128)(2,1)S(1)} %copy.440), channel_id=1, replica_groups=mesh['slab'=32,'coil'=8] {'slab'}, dimensions={2} | all-to-all | bytes 1048576 | tf_op jit(solution)/shard_map/all_to_all | solution.py:112
  406.4 17.0 %all_to_all.178 = f32[2,2,256,128]{3,1,0,2:T(2,128)} all-to-all(f32[2,2,256,128]{3,1,0,2:T(2,128)} %copy.444), channel_id=1, replica_groups=mesh['slab'=32,'coil'=8] {'coil'}, dimensions={2} | all-to-all | bytes 1048576 | tf_op jit(solution)/shard_map/all_to_all | solution.py:121
  424.7 12.8 %all_to_all.179 = f32[8,2,2,32,128]{4,3,2,1,0:T(8,128)S(1)} all-to-all(f32[8,2,2,32,128]{4,3,2,1,0:T(8,128)S(1)} %stack.210), channel_id=1, replica_groups=mesh['slab'=32,'coil'=8] {'coil'}, dimensions={0} | all-to-all | bytes 1048576 | tf_op jit(solution)/shard_map/all_to_all | solution.py:13
  448.9 19.7 %all_to_all.180 = bf16[2,2,2,256,128]{4,1,2,0,3:T(2,128)(2,1)S(1)} all-to-all(bf16[2,2,2,256,128]{4,1,2,0,3:T(2,128)(2,1)} %copy.449), channel_id=1, replica_groups=mesh['slab'=32,'coil'=8] {'slab'}, dimensions={3} | all-to-all | bytes 1048576 | tf_op jit(solution)/shard_map/all_to_all | solution.py:103
  471.9 21.2 %all_to_all.181 = bf16[2,2,64,8,128]{4,1,3,0,2:T(2,128)(2,1)S(1)} all-to-all(bf16[2,2,64,8,128]{4,1,3,0,2:T(2,128)(2,1)S(1)} %copy.453), channel_id=1, replica_groups=mesh['slab'=32,'coil'=8] {'slab'}, dimensions={2} | all-to-all | bytes 1048576 | tf_op jit(solution)/shard_map/all_to_all | solution.py:112
  497.6 17.0 %all_to_all.182 = f32[2,2,256,128]{3,1,0,2:T(2,128)} all-to-all(f32[2,2,256,128]{3,1,0,2:T(2,128)} %copy.457), channel_id=1, replica_groups=mesh['slab'=32,'coil'=8] {'coil'}, dimensions={2} | all-to-all | bytes 1048576 | tf_op jit(solution)/shard_map/all_to_all | solution.py:121
  517.9 19.9 %all_to_all.183 = f32[256,1,2]{2,1,0:T(1,128)} all-to-all(f32[256,1,2]{2,1,0:T(1,128)S(1)} %broadcast_in_dim.15), channel_id=1, replica_groups=mesh['slab'=32,'coil'=8] {'slab','coil'}, dimensions={0} | all-to-all | bytes 4096 | tf_op jit(solution)/shard_map/all_to_all | solution.py:134
  543.5 19.2 %all_to_all.184 = f32[256,1,1]{2,1,0:T(1,128)} all-to-all(f32[256,1,1]{2,1,0:T(1,128)S(1)} %broadcast_in_dim.16), channel_id=1, replica_groups=mesh['slab'=32,'coil'=8] {'slab','coil'}, dimensions={0} | all-to-all | bytes 2048 | tf_op jit(solution)/shard_map/all_to_all | solution.py:134
  566.9 12.8 %all_to_all.185 = f32[8,2,2,32,128]{4,3,2,1,0:T(8,128)S(1)} all-to-all(f32[8,2,2,32,128]{4,3,2,1,0:T(8,128)S(1)} %stack.217), channel_id=1, replica_groups=mesh['slab'=32,'coil'=8] {'coil'}, dimensions={0} | all-to-all | bytes 1048576 | tf_op jit(solution)/shard_map/all_to_all | solution.py:13
  591.1 19.6 %all_to_all.186 = bf16[2,2,2,256,128]{4,1,2,0,3:T(2,128)(2,1)S(1)} all-to-all(bf16[2,2,2,256,128]{4,1,2,0,3:T(2,128)(2,1)} %copy.464), channel_id=1, replica_groups=mesh['slab'=32,'coil'=8] {'slab'}, dimensions={3} | all-to-all | bytes 1048576 | tf_op jit(solution)/shard_map/all_to_all | solution.py:103
  614.1 20.9 %all_to_all.187 = bf16[2,2,64,8,128]{4,1,3,0,2:T(2,128)(2,1)S(1)} all-to-all(bf16[2,2,64,8,128]{4,1,3,0,2:T(2,128)(2,1)S(1)} %copy.468), channel_id=1, replica_groups=mesh['slab'=32,'coil'=8] {'slab'}, dimensions={2} | all-to-all | bytes 1048576 | tf_op jit(solution)/shard_map/all_to_all | solution.py:112
  636.8 15.4 %all_to_all.188 = f32[2,2,256,128]{3,1,0,2:T(2,128)S(1)} all-to-all(f32[2,2,256,128]{3,1,0,2:T(2,128)S(1)} %copy.472), channel_id=1, replica_groups=mesh['slab'=32,'coil'=8] {'coil'}, dimensions={2} | all-to-all | bytes 1048576 | tf_op jit(solution)/shard_map/all_to_all | solution.py:121
  654.4 6.4 all-to-all-start.14
  661.1 12.6 %all-to-all-done.14 = f32[256,1,1]{2,1,0:T(1,128)S(1)} async-done(((f32[256,1,1]{2,1,0:T(1,128)}), f32[256,1,1]{2,1,0:T(1,128)S(1)}, u32[]{:S(2)}, u32[]{:S(2)}) %all-to-all-start.14) | async-done | bytes 1056 | tf_op jit(solution)/shard_map/all_to_all | solution.py:134
  (200 shorter events, 213.8 us)
Async XLA Ops:
  0.6 361.9 %copy-start = (f32[2,2,64,8,128]{4,3,2,1,0:T(8,128)S(1)}, f32[2,2,64,8,128]{4,3,2,1,0:T(8,128)}, u32[]{:S(2)}) copy-start(f32[2,2,64,8,128]{4,3,2,1,0:T(8,128)} %param.16) | copy-start | bytes 3145732
  1.6 5.9 collective-permute-start
  5.5 4.5 collective-permute-start.1
  10.0 8.1 %collective-permute-start.2 = (bf16[2,4,1,128]{3,2,1,0:T(2,128)(2,1)S(1)}, bf16[2,4,1,128]{3,2,1,0:T(2,128)(2,1)S(1)}, u32[]{:S(2)}, u32[]{:S(2)}) collective-permute-start(bf16[2,4,1,128]{3,2,1,0:T(2,128)(2,1)S(1)} %get-tuple-element.62), channel_id=1, source_target_pairs={{0,1},{1,2},{2,3},{3,4},{4,5},{5,6},{6,7},{8,9},{9,10},{10,11},{11... | collective-permute-start | bytes 6152 | tf_op jit(solution)/shard_map/ppermute | solution.py:26
  15.2 4.9 collective-permute-start.3
  36.8 8.8 %collective-permute-start.4 = (bf16[32,1,32,128]{3,2,1,0:T(8,128)(2,1)S(1)}, bf16[32,1,32,128]{3,2,1,0:T(8,128)(2,1)}, u32[]{:S(2)}, u32[]{:S(2)}) collective-permute-start(bf16[32,1,32,128]{3,2,1,0:T(8,128)(2,1)S(1)} %copy.410), channel_id=1, source_target_pairs={{0,8},{8,16},{16,24},{24,32},{32,40},{40,48},{48,56},{56,64},{64,7... | collective-permute-start | bytes 786440 | tf_op jit(solution)/shard_map/ppermute | solution.py:26
  44.3 9.1 %collective-permute-start.5 = (bf16[32,1,32,128]{3,2,1,0:T(8,128)(2,1)}, bf16[32,1,32,128]{3,2,1,0:T(8,128)(2,1)}, u32[]{:S(2)}, u32[]{:S(2)}) collective-permute-start(bf16[32,1,32,128]{3,2,1,0:T(8,128)(2,1)} %copy.411), channel_id=1, source_target_pairs={{8,0},{16,8},{24,16},{32,24},{40,32},{48,40},{56,48},{64,56},{72,6... | collective-permute-start | bytes 786440 | tf_op jit(solution)/shard_map/ppermute | solution.py:28
  58.9 7.4 %collective-permute-start.6 = (bf16[32,4,1,128]{0,2,3,1:T(2,128)(2,1)S(1)}, bf16[32,4,1,128]{0,2,3,1:T(2,128)(2,1)S(1)}, u32[]{:S(2)}, u32[]{:S(2)}) collective-permute-start(bf16[32,4,1,128]{0,2,3,1:T(2,128)(2,1)S(1)} %get-tuple-element.28), channel_id=1, source_target_pairs={{0,1},{1,2},{2,3},{3,4},{4,5},{5,6},{6,7},{8,9},{9,10},{10,11},{11... | collective-permute-start | bytes 98312 | tf_op jit(solution)/shard_map/ppermute | solution.py:26
  63.0 7.7 %collective-permute-start.7 = (bf16[32,4,1,128]{0,2,3,1:T(2,128)(2,1)S(1)}, bf16[32,4,1,128]{0,2,3,1:T(2,128)(2,1)S(1)}, u32[]{:S(2)}, u32[]{:S(2)}) collective-permute-start(bf16[32,4,1,128]{0,2,3,1:T(2,128)(2,1)S(1)} %get-tuple-element.29), channel_id=1, source_target_pairs={{1,0},{2,1},{3,2},{4,3},{5,4},{6,5},{7,6},{9,8},{10,9},{11,10},{12... | collective-permute-start | bytes 98312 | tf_op jit(solution)/shard_map/ppermute | solution.py:28
  114.8 9.1 %collective-permute-start.8 = (bf16[32,1,32,128]{3,2,1,0:T(8,128)(2,1)S(1)}, bf16[32,1,32,128]{3,2,1,0:T(8,128)(2,1)}, u32[]{:S(2)}, u32[]{:S(2)}) collective-permute-start(bf16[32,1,32,128]{3,2,1,0:T(8,128)(2,1)S(1)} %copy.418), channel_id=1, source_target_pairs={{0,8},{8,16},{16,24},{24,32},{32,40},{40,48},{48,56},{56,64},{64,7... | collective-permute-start | bytes 786440 | tf_op jit(solution)/shard_map/ppermute | solution.py:26
  122.6 7.4 %collective-permute-start.9 = (bf16[32,1,32,128]{3,2,1,0:T(8,128)(2,1)}, bf16[32,1,32,128]{3,2,1,0:T(8,128)(2,1)}, u32[]{:S(2)}, u32[]{:S(2)}) collective-permute-start(bf16[32,1,32,128]{3,2,1,0:T(8,128)(2,1)} %copy.419), channel_id=1, source_target_pairs={{8,0},{16,8},{24,16},{32,24},{40,32},{48,40},{56,48},{64,56},{72,6... | collective-permute-start | bytes 786440 | tf_op jit(solution)/shard_map/ppermute | solution.py:28
  136.2 8.7 %collective-permute-start.10 = (bf16[32,4,1,128]{0,2,3,1:T(2,128)(2,1)}, bf16[32,4,1,128]{0,2,3,1:T(2,128)(2,1)S(1)}, u32[]{:S(2)}, u32[]{:S(2)}) collective-permute-start(bf16[32,4,1,128]{0,2,3,1:T(2,128)(2,1)} %get-tuple-element.26), channel_id=1, source_target_pairs={{0,1},{1,2},{2,3},{3,4},{4,5},{5,6},{6,7},{8,9},{9,10},{10,11},{11... | collective-permute-start | bytes 98312 | tf_op jit(solution)/shard_map/ppermute | solution.py:26
  141.3 8.0 %collective-permute-start.11 = (bf16[32,4,1,128]{0,2,3,1:T(2,128)(2,1)}, bf16[32,4,1,128]{0,2,3,1:T(2,128)(2,1)}, u32[]{:S(2)}, u32[]{:S(2)}) collective-permute-start(bf16[32,4,1,128]{0,2,3,1:T(2,128)(2,1)} %get-tuple-element.27), channel_id=1, source_target_pairs={{1,0},{2,1},{3,2},{4,3},{5,4},{6,5},{7,6},{9,8},{10,9},{11,10},{12... | collective-permute-start | bytes 98312 | tf_op jit(solution)/shard_map/ppermute | solution.py:28
  178.7 139.9 %copy-start.15 = (f32[2,2,32,128]{3,2,1,0:T(8,128)S(1)}, f32[2,2,32,128]{3,2,1,0:T(8,128)}, u32[]{:S(2)}) copy-start(f32[2,2,32,128]{3,2,1,0:T(8,128)} %param.9) | copy-start | bytes 196612
  320.1 12.9 %all-to-all-start = ((f32[8,2,2,32,128]{4,3,2,1,0:T(8,128)}), f32[8,2,2,32,128]{4,3,2,1,0:T(8,128)}, u32[]{:S(2)}, u32[]{:S(2)}) async-start(f32[8,2,2,32,128]{4,3,2,1,0:T(8,128)} %stack.91), calls=%async_computation | async-start | bytes 1048576 | tf_op jit(solution)/shard_map/all_to_all | solution.py:13
  334.9 25.4 %copy-start.16 = (s32[64,8]{0,1:T(8,128)S(1)}, s32[64,8]{0,1:T(8,128)}, u32[]{:S(2)}) copy-start(s32[64,8]{0,1:T(8,128)} %param.17) | copy-start | bytes 6148
  345.5 30.2 %all-to-all-start.1 = ((bf16[2,2,2,256,128]{4,1,2,0,3:T(2,128)(2,1)}), bf16[2,2,2,256,128]{4,1,2,0,3:T(2,128)(2,1)}, u32[]{:S(2)}, u32[]{:S(2)}) async-start(bf16[2,2,2,256,128]{4,1,2,0,3:T(2,128)(2,1)} %copy.436), calls=%async_computation.1 | async-start | bytes 1048576 | tf_op jit(solution)/shard_map/all_to_all | solution.py:103
  362.5 106.3 %copy-start.5 = (f32[1,64,2,64]{3,1,2,0:T(8,128)}, f32[1,64,2,64]{3,1,2,0:T(8,128)S(1)}, u32[]{:S(2)}) copy-start(f32[1,64,2,64]{3,1,2,0:T(8,128)S(1)} %get-tuple-element.57) | copy-start | bytes 98308
  448.9 21.4 %copy-start.8 = (f32[1,64,2,64]{3,1,2,0:T(8,128)S(1)}, f32[1,64,2,64]{3,1,2,0:T(8,128)}, u32[]{:S(2)}) copy-start(f32[1,64,2,64]{3,1,2,0:T(8,128)} %get-tuple-element.56) | copy-start | bytes 98308
  448.9 21.4 %copy-start.11 = (f32[1,64,2,64]{3,1,2,0:T(8,128)S(1)}, f32[1,64,2,64]{3,1,2,0:T(8,128)}, u32[]{:S(2)}) copy-start(f32[1,64,2,64]{3,1,2,0:T(8,128)} %get-tuple-element.65) | copy-start | bytes 98308
  515.8 48.8 %copy-start.4 = (f32[2,2,32,128]{3,1,0,2:T(2,128)}, f32[2,2,32,128]{3,1,0,2:T(2,128)S(1)}, u32[]{:S(2)}) copy-start(f32[2,2,32,128]{3,1,0,2:T(2,128)S(1)} %reduce_sum.150) | copy-start | bytes 196612
  591.1 21.2 %copy-start.12 = (f32[1,64,2,64]{3,1,2,0:T(8,128)S(1)}, f32[1,64,2,64]{3,1,2,0:T(8,128)}, u32[]{:S(2)}) copy-start(f32[1,64,2,64]{3,1,2,0:T(8,128)} %get-tuple-element.65) | copy-start | bytes 98308
  636.2 39.7 %copy-start.14 = (f32[2,2,32,128]{3,1,0,2:T(2,128)S(1)}, f32[2,2,32,128]{3,1,0,2:T(2,128)}, u32[]{:S(2)}) copy-start(f32[2,2,32,128]{3,1,0,2:T(2,128)} %copy-done.13) | copy-start | bytes 196612
  654.4 19.4 %all-to-all-start.14 = ((f32[256,1,1]{2,1,0:T(1,128)}), f32[256,1,1]{2,1,0:T(1,128)S(1)}, u32[]{:S(2)}, u32[]{:S(2)}) async-start(f32[256,1,1]{2,1,0:T(1,128)} %broadcast_in_dim.17), calls=%async_computation.14 | async-start | bytes 262144 | tf_op jit(solution)/shard_map/all_to_all | solution.py:134
  (13 other events, 134.6 us)
